TPU v7x, 32 devices: a whole 2x2x4 slice. The times are simulated.
32 devices in a mesh: groups: 2 (over y), area: 4 (over z), neuron: 4 (over x, core).
Axes of the slice: x: 2, y: 2, z: 4, core: 2. Of those that a mesh axis runs over, the one named last changes fastest.
Arguments:
- window: bfloat16 [32, 16, 32768], P(None, 'groups', ('area', 'neuron')), parts along dimension 1, may hold values from -6 to 6
- err_grad: float32 [16, 16, 32768], P(None, 'groups', ('area', 'neuron')), parts along dimension 1, may hold values from -6 to 6
- surrogate: float32 [16, 16, 32768], P(None, 'groups', ('area', 'neuron')), parts along dimension 1, may hold values from 0 to 0.5
- lv_end: float32 [16, 32768], P('groups', ('area', 'neuron')), parts along dimension 0, may hold values from -6 to 6
- la_end: float32 [16, 32768], P('groups', ('area', 'neuron')), parts along dimension 0, may hold values from -6 to 6
- alpha: float32 [32768], P(('area', 'neuron')), may hold values from 0.8 to 0.99
- rho: float32 [32768], P(('area', 'neuron')), may hold values from 0.9 to 0.999
- beta: float32 [32768], P(('area', 'neuron')), may hold values from 0.3 to 2
- weights: bfloat16 [4, 4, 64, 4, 128, 128], P(None, 'area', 'neuron'), may hold values from -0.25 to 0.25
- block_index: int32 [4, 4, 64, 4], P(None, 'area', 'neuron'), may hold values from 0 to 63, as said below
- delays: int32 [4, 4], replicated, may hold values from 16 to 31, as said below
Outputs:
- cur_adjoint: bfloat16 [16, 16, 32768], P(None, 'groups', ('area', 'neuron')), parts along dimension 1
- lv_start: float32 [16, 32768], P('groups', ('area', 'neuron')), parts along dimension 0
- la_start: float32 [16, 32768], P('groups', ('area', 'neuron')), parts along dimension 0
There are 2 independent parts, one for each index of `groups`. A program takes and returns all parts, laid end to end along the dimension named above; an argument that names none is the same for every part. Nothing has to cross between parts.
Inputs may be any that keep to these rules, and one draw needn't show every extreme that they name: `delays`: every entry lies in 16 to 31 and both ends occur. `block_index`: both ends occur.
All inputs are finite; a program needn't handle non-finite values.
Results may differ from a plain program's by a relative error of at most 0.001.
Values may be sent and summed in bfloat16 or wider, within the bound.
No kernel may reach another device: no remote copies, remote signals or barrier semaphores. Data moves between devices by JAX's collectives and lax.ppermute only.
A program may use at most 64 MiB of HBM per device.

v0:
```python
import jax
import jax.numpy as jnp
from jax import lax
from jax.sharding import PartitionSpec as P


def partner(value, axis, bit):
    mask = 2**bit
    pairs = [(source, source ^ mask) for source in range(lax.axis_size(axis))]
    return lax.ppermute(value, axis, pairs)


def adjoint_scan(err_grad, surrogate, rec, lv_end, la_end, alpha, rho, beta):

    def step(carry, inputs):
        lv_now, la_now = carry
        error_t, surr_t, rec_t = inputs
        total = error_t + rec_t - lv_now + la_now
        lv_next = alpha * lv_now + surr_t * total
        la_next = rho * la_now - beta * surr_t * total
        return ((lv_next, la_next), lv_now.astype(jnp.bfloat16))

    (lv_start, la_start), currents = lax.scan(
        step, (lv_end, la_end), (err_grad, surrogate, rec), reverse=True
    )
    return (currents, lv_start, la_start)


def per_device(
    window, err_grad, surrogate, lv_end, la_end, alpha, rho, beta, weights, block_index, delays
):
    steps = err_grad.shape[0]
    batch = err_grad.shape[1]
    local_neurons = err_grad.shape[2]
    block_side = weights.shape[-1]
    rounds = weights.shape[0]
    levels = lax.axis_size("area").bit_length() - 1
    me_area = lax.axis_index("area")
    rec = jnp.zeros((steps * batch, local_neurons), jnp.float32)
    for rnd in range(rounds):
        bit = rnd % levels
        arrived = partner(window, "area", bit)
        start = delays[rnd, me_area] - steps
        used = lax.dynamic_slice_in_dim(arrived, start, steps, 0)
        panel = lax.all_gather(used, "neuron", axis=2, tiled=True)
        flat = panel.reshape(steps * batch, panel.shape[2] // block_side, block_side)
        picked = jnp.take(flat, block_index[rnd, 0], axis=1)
        contrib = jnp.einsum(
            "rjkc,jkcd->rjd", picked, weights[rnd, 0], preferred_element_type=jnp.float32
        )
        rec = rec + contrib.reshape(steps * batch, local_neurons)
    rec = rec.reshape(steps, batch, local_neurons)
    return adjoint_scan(err_grad, surrogate, rec, lv_end, la_end, alpha, rho, beta)


def solution(mesh):
    placed = (
        P(None, "groups", ("area", "neuron")),
        P(None, "groups", ("area", "neuron")),
        P(None, "groups", ("area", "neuron")),
        P("groups", ("area", "neuron")),
        P("groups", ("area", "neuron")),
        P(("area", "neuron")),
        P(("area", "neuron")),
        P(("area", "neuron")),
        P(None, "area", "neuron", None, None, None),
        P(None, "area", "neuron", None),
        P(),
    )
    return jax.shard_map(
        per_device,
        mesh=mesh,
        in_specs=placed,
        out_specs=(
            P(None, "groups", ("area", "neuron")),
            P("groups", ("area", "neuron")),
            P("groups", ("area", "neuron")),
        ),
        check_vma=False,
    )
```

profile of v0, /device:TPU:0, one launch (start us, length us, event | category | flops | bytes accessed | tf_op | source)
XLA Modules:
  0.0 206.2 jit_solution(3993261804340114842)
XLA Ops:
  7.2 3.1 %collective-permute-start = (bf16[32,8,2048]{2,1,0:T(8,128)(2,1)}, bf16[32,8,2048]{2,1,0:T(8,128)(2,1)S(1)}, u32[]{:S(2)}, u32[]{:S(2)}) collective-permute-start(bf16[32,8,2048]{2,1,0:T(8,128)(2,1)} %param.15), channel_id=1, source_target_pairs={{0,4},{4,0},{8,12},{12,8},{1,5},{5,1},{9,13},{13,9},{2,6},{6,2},{1... | collective-permute-start | bytes 3145736 | tf_op jit(solution)/shard_map/ppermute | solution.py:10
  10.3 1.5 constant_dynamic-slice_fusion.5
  14.4 19.3 %collective-permute-done = bf16[32,8,2048]{2,1,0:T(8,128)(2,1)S(1)} collective-permute-done((bf16[32,8,2048]{2,1,0:T(8,128)(2,1)}, bf16[32,8,2048]{2,1,0:T(8,128)(2,1)S(1)}, u32[]{:S(2)}, u32[]{:S(2)}) %collective-permute-start) | collective-permute-done | bytes 1048608 | tf_op jit(solution)/shard_map/ppermute | solution.py:10
  34.9 2.8 %collective-permute-start.1 = (bf16[32,8,2048]{2,1,0:T(8,128)(2,1)S(1)}, bf16[32,8,2048]{2,1,0:T(8,128)(2,1)S(1)}, u32[]{:S(2)}, u32[]{:S(2)}) collective-permute-start(bf16[32,8,2048]{2,1,0:T(8,128)(2,1)S(1)} %copy-done.12), channel_id=1, source_target_pairs={{0,8},{4,12},{8,0},{12,4},{1,9},{5,13},{9,1},{13,5},{2,10},{6,14},... | collective-permute-start | bytes 3145736 | tf_op jit(solution)/shard_map/ppermute | solution.py:10
  40.1 42.5 %collective-permute-done.1 = bf16[32,8,2048]{2,1,0:T(8,128)(2,1)S(1)} collective-permute-done((bf16[32,8,2048]{2,1,0:T(8,128)(2,1)S(1)}, bf16[32,8,2048]{2,1,0:T(8,128)(2,1)S(1)}, u32[]{:S(2)}, u32[]{:S(2)}) %collective-permute-start.1) | collective-permute-done | bytes 1048608 | tf_op jit(solution)/shard_map/ppermute | solution.py:10
  86.2 2.2 %copy.52 = bf16[16,8,64,128]{3,2,1,0:T(8,128)(2,1)S(1)} copy(bf16[16,8,64,128]{3,1,2,0:T(8,128)(2,1)} %bitcast.147) | data formatting | bytes 4194304
  89.8 17.6 %all-gather.7.cloned.1.call-done = bf16[16,8,8192]{2,1,0:T(8,128)(2,1)} async-done(((bf16[16,8,2048]{2,1,0:T(8,128)(2,1)}), bf16[16,8,8192]{2,1,0:T(8,128)(2,1)}) %all-gather.7.cloned.1.call-update) | async-done | bytes 2097168 | tf_op jit(solution)/shard_map/all_gather | solution.py:45
  107.4 2.2 %copy.53 = bf16[16,8,64,128]{3,2,1,0:T(8,128)(2,1)S(1)} copy(bf16[16,8,64,128]{3,1,2,0:T(8,128)(2,1)} %bitcast.148) | data formatting | bytes 4194304
  109.6 2.7 %copy.40 = bf16[128,64,128]{2,0,1:T(8,128)(2,1)} copy(bf16[128,64,128]{2,1,0:T(8,128)(2,1)S(1)} %bitcast.144) | data formatting | bytes 4194304 | tf_op jit(solution)/shard_map/reshape | solution.py:46
  112.3 19.9 %all-gather.9.cloned.1.call-done = bf16[16,8,8192]{2,1,0:T(8,128)(2,1)} async-done(((bf16[16,8,2048]{2,1,0:T(8,128)(2,1)}), bf16[16,8,8192]{2,1,0:T(8,128)(2,1)}) %all-gather.9.cloned.1.call-update) | async-done | bytes 2097168 | tf_op jit(solution)/shard_map/all_gather | solution.py:45
  132.2 2.2 %copy.54 = bf16[16,8,64,128]{3,2,1,0:T(8,128)(2,1)S(1)} copy(bf16[16,8,64,128]{3,1,2,0:T(8,128)(2,1)} %bitcast.149) | data formatting | bytes 4194304
  134.4 2.7 %copy.43 = bf16[128,64,128]{2,0,1:T(8,128)(2,1)} copy(bf16[128,64,128]{2,1,0:T(8,128)(2,1)S(1)} %bitcast.145) | data formatting | bytes 4194304 | tf_op jit(solution)/shard_map/reshape | solution.py:46
  137.1 19.1 %all-gather.11.cloned.1.call-done = bf16[16,8,8192]{2,1,0:T(8,128)(2,1)} async-done(((bf16[16,8,2048]{2,1,0:T(8,128)(2,1)}), bf16[16,8,8192]{2,1,0:T(8,128)(2,1)}) %all-gather.11.cloned.1.call-update) | async-done | bytes 2097168 | tf_op jit(solution)/shard_map/all_gather | solution.py:45
  156.2 2.2 %copy.55 = bf16[16,8,64,128]{3,2,1,0:T(8,128)(2,1)S(1)} copy(bf16[16,8,64,128]{3,1,2,0:T(8,128)(2,1)} %bitcast.150) | data formatting | bytes 4194304
  158.4 2.7 %copy.46 = bf16[128,64,128]{2,0,1:T(8,128)(2,1)} copy(bf16[128,64,128]{2,1,0:T(8,128)(2,1)S(1)} %bitcast.146) | data formatting | bytes 4194304 | tf_op jit(solution)/shard_map/reshape | solution.py:46
  161.1 2.1 %gather_fusion = bf16[64,128,128]{2,1,0:T(8,128)(2,1)} fusion(bf16[128,64,128]{2,0,1:T(8,128)(2,1)S(1)} %copy.37, s32[1024]{0:T(1024)S(1)} %pad_clamp_fusion.3), kind=kCustom, calls=%fused_computation.clone | custom fusion | bytes 4194560 | tf_op jit(solution)/shard_map/jit(_take)/gather | solution.py:47
  163.3 4.0 %gather_fusion.1 = bf16[64,128,128]{2,1,0:T(8,128)(2,1)} fusion(bf16[128,64,128]{2,0,1:T(8,128)(2,1)} %copy.40, s32[1024]{0:T(1024)S(1)} %pad_clamp_fusion.2), kind=kCustom, calls=%fused_computation.1.clone | custom fusion | bytes 4194560 | tf_op jit(solution)/shard_map/jit(_take)/gather | solution.py:47
  167.2 2.2 %gather_fusion.2 = bf16[64,128,128]{2,1,0:T(8,128)(2,1)} fusion(bf16[128,64,128]{2,0,1:T(8,128)(2,1)S(1)} %copy-done, s32[1024]{0:T(1024)S(1)} %pad_clamp_fusion.1), kind=kCustom, calls=%fused_computation.2.clone | custom fusion | bytes 4194560 | tf_op jit(solution)/shard_map/jit(_take)/gather | solution.py:47
  169.4 2.5 %gather_fusion.3 = bf16[64,128,128]{2,1,0:T(8,128)(2,1)S(1)} fusion(bf16[128,64,128]{2,0,1:T(8,128)(2,1)} %copy.46, s32[1024]{0:T(1024)S(1)} %pad_clamp_fusion), kind=kCustom, calls=%fused_computation.3.clone | custom fusion | bytes 4194560 | tf_op jit(solution)/shard_map/jit(_take)/gather | solution.py:47
  172.0 3.1 %fusion.28 = f32[16,128,128]{2,1,0:T(8,128)S(1)} fusion(bf16[4,1,16,4,128,128]{5,4,3,2,1,0:T(8,128)(2,1)} %param.23, bf16[16,4,128,128]{3,2,1,0:T(8,128)(2,1)} %bitcast.153, pred[16,4]{1,0:T(8,128)(4,1)S(1)} %copy.35), kind=kOutput, calls=%fused_computation.36 | convolution fusion | flops 269484032 | bytes 5242944 | tf_op jit(solution)/shard_map/rjkc,jkcd->rjd/dot_general | solution.py:48
  175.1 2.5 %fusion.63 = f32[16,128,128]{2,1,0:T(8,128)S(1)} fusion(f32[16,128,128]{2,1,0:T(8,128)S(1)} %fusion.28, bf16[4,1,16,4,128,128]{5,4,3,2,1,0:T(8,128)(2,1)} %param.23, bf16[16,4,128,128]{3,2,1,0:T(8,128)(2,1)S(1)} %bitcast.154, pred[16,4]{1,0:T(8,128)(4,1)S(1)} %copy.38), kind=kOutput, calls=%fused_computation.43 | convolution fusion | flops 269746176 | bytes 6291520 | tf_op jit(solution)/shard_map/rjkc,jkcd->rjd/dot_general | solution.py:48
  177.6 2.4 %fusion.58 = f32[16,128,128]{2,1,0:T(8,128)S(1)} fusion(f32[16,128,128]{2,1,0:T(8,128)S(1)} %fusion.63, bf16[4,1,16,4,128,128]{5,4,3,2,1,0:T(8,128)(2,1)} %param.23, bf16[16,4,128,128]{3,2,1,0:T(8,128)(2,1)S(1)} %bitcast.152, pred[16,4]{1,0:T(8,128)(4,1)S(1)} %copy.41), kind=kOutput, calls=%fused_computation.42 | convolution fusion | flops 269746176 | bytes 6291520 | tf_op jit(solution)/shard_map/rjkc,jkcd->rjd/dot_general | solution.py:48
  180.0 2.4 %fusion.53 = f32[128,16,128]{2,0,1:T(8,128)S(1)} fusion(f32[16,128,128]{2,1,0:T(8,128)S(1)} %fusion.58, bf16[4,1,16,4,128,128]{5,4,3,2,1,0:T(8,128)(2,1)} %param.23, bf16[16,4,128,128]{3,2,1,0:T(8,128)(2,1)S(1)} %bitcast.151, pred[16,4]{1,0:T(8,128)(4,1)S(1)} %copy.44), kind=kOutput, calls=%fused_computation.41 | convolution fusion | flops 269746176 | bytes 6291520 | tf_op jit(solution)/shard_map/rjkc,jkcd->rjd/dot_general | solution.py:48
  183.4 15.5 %while.18 = (s32[]{:T(128)}, f32[8,2048]{1,0:T(8,128)S(1)}, f32[8,2048]{1,0:T(8,128)S(1)}, bf16[16,8,2048]{2,1,0:T(8,128)(2,1)S(1)}, f32[2048]{0:T(1024)S(1)}, /...) while((s32[]{:T(128)}, f32[8,2048]{1,0:T(8,128)S(1)}, ...), condition=%wide.region_1.3_spmd, body=%wide.region_0.0_spmd.sunk | while | flops 180227 | bytes 581769 | solution.py:23
  (91 shorter events, 22.8 us)
Async XLA Ops:
  7.2 27.7 %copy-start.12 = (bf16[32,8,2048]{2,1,0:T(8,128)(2,1)S(1)}, bf16[32,8,2048]{2,1,0:T(8,128)(2,1)}, u32[]{:S(2)}) copy-start(bf16[32,8,2048]{2,1,0:T(8,128)(2,1)} %param.15) | copy-start | bytes 3145732
  7.2 79.0 %all-gather.5.cloned.1.call-start = ((), (), s32[]{:S(2)}) async-start(), calls=%async_computation | async-start | bytes 2621440 | tf_op jit(solution)/shard_map/all_gather | solution.py:45
  7.2 26.5 %collective-permute-start = (bf16[32,8,2048]{2,1,0:T(8,128)(2,1)}, bf16[32,8,2048]{2,1,0:T(8,128)(2,1)S(1)}, u32[]{:S(2)}, u32[]{:S(2)}) collective-permute-start(bf16[32,8,2048]{2,1,0:T(8,128)(2,1)} %param.15), channel_id=1, source_target_pairs={{0,4},{4,0},{8,12},{12,8},{1,5},{5,1},{9,13},{13,9},{2,6},{6,2},{1... | collective-permute-start | bytes 3145736 | tf_op jit(solution)/shard_map/ppermute | solution.py:10
  34.8 50.2 %copy-start.11 = (s32[4,1,16,4]{2,3,1,0:T(4,128)S(1)}, s32[4,1,16,4]{2,3,1,0:T(4,128)}, u32[]{:S(2)}) copy-start(s32[4,1,16,4]{2,3,1,0:T(4,128)} %param.24) | copy-start | bytes 3076
  34.8 72.6 %all-gather.7.cloned.1.call-start = ((), (), s32[]{:S(2)}) async-start(), calls=%async_computation.1 | async-start | bytes 2621440 | tf_op jit(solution)/shard_map/all_gather | solution.py:45
  34.9 47.8 %collective-permute-start.1 = (bf16[32,8,2048]{2,1,0:T(8,128)(2,1)S(1)}, bf16[32,8,2048]{2,1,0:T(8,128)(2,1)S(1)}, u32[]{:S(2)}, u32[]{:S(2)}) collective-permute-start(bf16[32,8,2048]{2,1,0:T(8,128)(2,1)S(1)} %copy-done.12), channel_id=1, source_target_pairs={{0,8},{4,12},{8,0},{12,4},{1,9},{5,13},{9,1},{13,5},{2,10},{6,14},... | collective-permute-start | bytes 3145736 | tf_op jit(solution)/shard_map/ppermute | solution.py:10
  83.7 48.5 %all-gather.9.cloned.1.call-start = ((), (), s32[]{:S(2)}) async-start(), calls=%async_computation.2 | async-start | bytes 2621440 | tf_op jit(solution)/shard_map/all_gather | solution.py:45
  84.4 71.8 %all-gather.11.cloned.1.call-start = ((), (), s32[]{:S(2)}) async-start(), calls=%async_computation.3 | async-start | bytes 2621440 | tf_op jit(solution)/shard_map/all_gather | solution.py:45
  163.3 4.0 %copy-start = (bf16[128,64,128]{2,0,1:T(8,128)(2,1)S(1)}, bf16[128,64,128]{2,0,1:T(8,128)(2,1)}, u32[]{:S(2)}) copy-start(bf16[128,64,128]{2,0,1:T(8,128)(2,1)} %copy.43) | copy-start | bytes 6291460
  171.9 3.1 %copy-start.6 = (bf16[64,128,128]{2,1,0:T(8,128)(2,1)S(1)}, bf16[64,128,128]{2,1,0:T(8,128)(2,1)}, u32[]{:S(2)}) copy-start(bf16[64,128,128]{2,1,0:T(8,128)(2,1)} %gather_fusion.1) | copy-start | bytes 6291460
  175.1 2.6 %copy-start.5 = (bf16[64,128,128]{2,1,0:T(8,128)(2,1)S(1)}, bf16[64,128,128]{2,1,0:T(8,128)(2,1)}, u32[]{:S(2)}) copy-start(bf16[64,128,128]{2,1,0:T(8,128)(2,1)} %gather_fusion.2) | copy-start | bytes 6291460
  182.4 0.9 copy-start.2
  182.5 0.9 copy-start.4
  182.5 0.9 copy-start.8
  182.5 0.9 copy-start.9
  182.5 0.9 copy-start.10
  198.8 0.6 copy-start.1
  198.9 0.6 copy-start.3
  198.9 0.8 copy-start.7
Sparse Core Ops, SparseCore 0:
  34.9 23.9 all-gather.4
  83.8 23.5 all-gather.6
  109.6 22.5 all-gather.8
  133.6 22.5 all-gather.10
where the time goes:
time: 207 us; the launch traced here: 206 us
  waiting for transfers between devices  120 us (58%)
  local copies, waits for them, and re-layouts  35.4 us (17%)
  between operations  19.1 us (9%)
  other arithmetic  15.2 us (7%)
  matrix products  10.4 us (5%)
  starting transfers between devices  6.07 us (3%)
    ppermute x2, waiting for transfers between devices, partner(): return lax.ppermute(value, axis, pairs)  61.8 us
    all_gather x4, waiting for transfers between devices, per_device(): panel = lax.all_gather(used, 'neuron', axis=2, tiled=True)  56.6 us
    sub x16, other arithmetic, step(): la_next = rho * la_now - beta * surr_t * total  15 us
    gather x4, local copies, waits for them, and re-layouts, per_device(): picked = jnp.take(flat, block_index[rnd, 0], axis=1)  10.8 us
    dot_general x4, matrix products, per_device(): jnp.einsum('rjkc,jkcd->rjd', picked, weights[rnd, 0], preferred_element_t...  10.4 us
    unnamed x30, local copies, waits for them, and re-layouts  9.6 us
    reshape x4, local copies, waits for them, and re-layouts, per_device(): panel.reshape(steps * batch, panel.shape[2] // block_side, block_side)  9.53 us
    ppermute x2, starting transfers between devices, partner(): return lax.ppermute(value, axis, pairs)  5.91 us
  transfers between devices with their start and end apart: 6, of which 5 were waited for; matrix products, arithmetic and copies ran while one was open for 8% of the time, Pallas kernels for 0%

commit v1 on v0

--- a/solution.py
+++ b/solution.py
@@ -42,7 +42,16 @@
         arrived = partner(window, "area", bit)
         start = delays[rnd, me_area] - steps
         used = lax.dynamic_slice_in_dim(arrived, start, steps, 0)
-        panel = lax.all_gather(used, "neuron", axis=2, tiled=True)
+        ring = [used]
+        for hop in range(3):
+            ring.append(
+                lax.ppermute(ring[-1], "neuron", [(dev, (dev + 1) % 4) for dev in range(4)])
+            )
+        panel = jnp.roll(
+            jnp.concatenate(ring[::-1], axis=2),
+            (lax.axis_index("neuron") + 1) * ring[0].shape[2],
+            axis=2,
+        )
         flat = panel.reshape(steps * batch, panel.shape[2] // block_side, block_side)
         picked = jnp.take(flat, block_index[rnd, 0], axis=1)
         contrib = jnp.einsum(

time: 207 us -> 173 us (0.84)
  waiting for transfers between devices: 120 us -> 86.5 us
  other arithmetic: 15.2 us -> 31.6 us
  between operations: 19.1 us -> 6.3 us
  local copies, waits for them, and re-layouts: 35.4 us -> 28.5 us
    all_gather x4 -> x0, waiting for transfers between devices: 56.6 us -> none  [per_device(): panel = lax.all_gather(used, 'neuron', axis=2, tiled=True)]
    ppermute x0 -> x12, waiting for transfers between devices: none -> 47.4 us  [per_device(): lax.ppermute(ring[-1], 'neuron', [(dev, (dev + 1) % 4) for dev in range(4)])]
    ppermute x2, waiting for transfers between devices: 61.8 us -> 39.1 us  [partner(): return lax.ppermute(value, axis, pairs)]
    unnamed x0 -> x4, other arithmetic: none -> 16.5 us
    unnamed x30 -> x40, local copies, waits for them, and re-layouts: 9.6 us -> 3.32 us
    ppermute x0 -> x12, starting transfers between devices: none -> 2.38 us  [per_device(): lax.ppermute(ring[-1], 'neuron', [(dev, (dev + 1) % 4) for dev in range(4)])]
  transfers between devices with their start and end apart: 6 -> 14, of which waited for: 5 -> 10; matrix products, arithmetic and copies ran while one was open for 8% -> 14% of each run, Pallas kernels for 0% -> 0%
where the time goes in v1:
time: 173 us; the launch traced here: 172 us
  waiting for transfers between devices  86.5 us (50%)
  other arithmetic  31.6 us (18%)
  local copies, waits for them, and re-layouts  28.5 us (16%)
  matrix products  10.4 us (6%)
  starting transfers between devices  8.05 us (5%)
  between operations  6.3 us (4%)
    ppermute x12, waiting for transfers between devices, per_device(): lax.ppermute(ring[-1], 'neuron', [(dev, (dev + 1) % 4) for dev in range(4)])  47.4 us
    ppermute x2, waiting for transfers between devices, partner(): return lax.ppermute(value, axis, pairs)  39.1 us
    unnamed x4, other arithmetic  16.5 us
    sub x16, other arithmetic, step(): la_next = rho * la_now - beta * surr_t * total  15 us
    gather x4, local copies, waits for them, and re-layouts, per_device(): picked = jnp.take(flat, block_index[rnd, 0], axis=1)  10.9 us
    dot_general x4, matrix products, per_device(): jnp.einsum('rjkc,jkcd->rjd', picked, weights[rnd, 0], preferred_element_t...  10.4 us
    reshape x4, local copies, waits for them, and re-layouts, per_device(): panel.reshape(steps * batch, panel.shape[2] // block_side, block_side)  9.52 us
    ppermute x2, starting transfers between devices, partner(): return lax.ppermute(value, axis, pairs)  5.68 us
  transfers between devices with their start and end apart: 14, of which 10 were waited for; matrix products, arithmetic and copies ran while one was open for 14% of the time, Pallas kernels for 0%

profile of v1, /device:TPU:0, one launch (start us, length us, event | category | flops | bytes accessed | tf_op | source)
XLA Modules:
  0.0 171.7 jit_solution(11676293428684791238)
XLA Ops:
  0.6 3.1 %collective-permute-start = (bf16[32,8,2048]{2,1,0:T(8,128)(2,1)}, bf16[32,8,2048]{2,1,0:T(8,128)(2,1)}, u32[]{:S(2)}, u32[]{:S(2)}) collective-permute-start(bf16[32,8,2048]{2,1,0:T(8,128)(2,1)} %param.17), channel_id=1, source_target_pairs={{0,4},{4,0},{8,12},{12,8},{1,5},{5,1},{9,13},{13,9},{2,6},{6,2},{1... | collective-permute-start | bytes 3145736 | tf_op jit(solution)/shard_map/ppermute | solution.py:10
  3.7 2.6 %collective-permute-start.4 = (bf16[32,8,2048]{2,1,0:T(8,128)(2,1)}, bf16[32,8,2048]{2,1,0:T(8,128)(2,1)S(1)}, u32[]{:S(2)}, u32[]{:S(2)}) collective-permute-start(bf16[32,8,2048]{2,1,0:T(8,128)(2,1)} %param.17), channel_id=1, source_target_pairs={{0,8},{4,12},{8,0},{12,4},{1,9},{5,13},{9,1},{13,5},{2,10},{6,14},... | collective-permute-start | bytes 3145736 | tf_op jit(solution)/shard_map/ppermute | solution.py:10
  10.4 39.1 %collective-permute-done = bf16[32,8,2048]{2,1,0:T(8,128)(2,1)} collective-permute-done((bf16[32,8,2048]{2,1,0:T(8,128)(2,1)}, bf16[32,8,2048]{2,1,0:T(8,128)(2,1)}, u32[]{:S(2)}, u32[]{:S(2)}) %collective-permute-start) | collective-permute-done | bytes 1048608 | tf_op jit(solution)/shard_map/ppermute | solution.py:10
  55.9 3.7 %collective-permute-done.1 = bf16[16,8,2048]{2,1,0:T(8,128)(2,1)} collective-permute-done((bf16[16,8,2048]{2,1,0:T(8,128)(2,1)S(1)}, bf16[16,8,2048]{2,1,0:T(8,128)(2,1)}, u32[]{:S(2)}, u32[]{:S(2)}) %collective-permute-start.1) | collective-permute-done | bytes 524320 | tf_op jit(solution)/shard_map/ppermute | solution.py:48
  59.6 5.6 %collective-permute-done.5 = bf16[16,8,2048]{2,1,0:T(8,128)(2,1)} collective-permute-done((bf16[16,8,2048]{2,1,0:T(8,128)(2,1)S(1)}, bf16[16,8,2048]{2,1,0:T(8,128)(2,1)}, u32[]{:S(2)}, u32[]{:S(2)}) %collective-permute-start.5) | collective-permute-done | bytes 524320 | tf_op jit(solution)/shard_map/ppermute | solution.py:48
  65.2 5.5 %collective-permute-done.8 = bf16[16,8,2048]{2,1,0:T(8,128)(2,1)S(1)} collective-permute-done((bf16[16,8,2048]{2,1,0:T(8,128)(2,1)S(1)}, bf16[16,8,2048]{2,1,0:T(8,128)(2,1)S(1)}, u32[]{:S(2)}, u32[]{:S(2)}) %collective-permute-start.8) | collective-permute-done | bytes 524320 | tf_op jit(solution)/shard_map/ppermute | solution.py:48
  70.7 5.6 %collective-permute-done.11 = bf16[16,8,2048]{2,1,0:T(8,128)(2,1)S(1)} collective-permute-done((bf16[16,8,2048]{2,1,0:T(8,128)(2,1)S(1)}, bf16[16,8,2048]{2,1,0:T(8,128)(2,1)S(1)}, u32[]{:S(2)}, u32[]{:S(2)}) %collective-permute-start.11) | collective-permute-done | bytes 524320 | tf_op jit(solution)/shard_map/ppermute | solution.py:48
  76.3 5.7 %collective-permute-done.2 = bf16[16,8,2048]{2,1,0:T(8,128)(2,1)} collective-permute-done((bf16[16,8,2048]{2,1,0:T(8,128)(2,1)}, bf16[16,8,2048]{2,1,0:T(8,128)(2,1)}, u32[]{:S(2)}, u32[]{:S(2)}) %collective-permute-start.2) | collective-permute-done | bytes 524320 | tf_op jit(solution)/shard_map/ppermute | solution.py:48
  83.2 4.4 %collective-permute-done.6 = bf16[16,8,2048]{2,1,0:T(8,128)(2,1)} collective-permute-done((bf16[16,8,2048]{2,1,0:T(8,128)(2,1)}, bf16[16,8,2048]{2,1,0:T(8,128)(2,1)}, u32[]{:S(2)}, u32[]{:S(2)}) %collective-permute-start.6) | collective-permute-done | bytes 524320 | tf_op jit(solution)/shard_map/ppermute | solution.py:48
  87.7 5.6 %collective-permute-done.9 = bf16[16,8,2048]{2,1,0:T(8,128)(2,1)} collective-permute-done((bf16[16,8,2048]{2,1,0:T(8,128)(2,1)S(1)}, bf16[16,8,2048]{2,1,0:T(8,128)(2,1)}, u32[]{:S(2)}, u32[]{:S(2)}) %collective-permute-start.9) | collective-permute-done | bytes 524320 | tf_op jit(solution)/shard_map/ppermute | solution.py:48
  93.3 5.6 %collective-permute-done.12 = bf16[16,8,2048]{2,1,0:T(8,128)(2,1)} collective-permute-done((bf16[16,8,2048]{2,1,0:T(8,128)(2,1)S(1)}, bf16[16,8,2048]{2,1,0:T(8,128)(2,1)}, u32[]{:S(2)}, u32[]{:S(2)}) %collective-permute-start.12) | collective-permute-done | bytes 524320 | tf_op jit(solution)/shard_map/ppermute | solution.py:48
  98.9 5.6 %collective-permute-done.3 = bf16[16,8,2048]{2,1,0:T(8,128)(2,1)} collective-permute-done((bf16[16,8,2048]{2,1,0:T(8,128)(2,1)}, bf16[16,8,2048]{2,1,0:T(8,128)(2,1)}, u32[]{:S(2)}, u32[]{:S(2)}) %collective-permute-start.3) | collective-permute-done | bytes 524320 | tf_op jit(solution)/shard_map/ppermute | solution.py:48
  104.5 4.0 %fusion.32 = bf16[16,8,64,128]{3,1,2,0:T(8,128)(2,1)S(1)} fusion(s32[]{:T(128)S(6)} %select_n.57, bf16[16,8,2048]{2,1,0:T(8,128)(2,1)} %collective-permute-done.3, bf16[16,8,2048]{2,1,0:T(8,128)(2,1)} %collective-permute-done.2, bf16[16,8,2048]{2,1,0:T(8,128)(2,1)} %collective-permute-done.1, bf16[16,8,2048]{2,1,0:T(8,128)(2,1)S(1)} %get-tuple-element.233), kind=kLoop, calls=%fused_computation.72 | loop fusion | flops 16777216 | bytes 4194308
  110.6 4.0 %fusion.24 = bf16[16,8,64,128]{3,1,2,0:T(8,128)(2,1)S(1)} fusion(s32[]{:T(128)S(6)} %select_n.57, bf16[16,8,2048]{2,1,0:T(8,128)(2,1)S(1)} %collective-permute-done.7, bf16[16,8,2048]{2,1,0:T(8,128)(2,1)} %collective-permute-done.6, bf16[16,8,2048]{2,1,0:T(8,128)(2,1)} %collective-permute-done.5, bf16[16,8,2048]{2,1,0:T(8,128)(2,1)S(1)} %copy-done.8), kind=kLoop, calls=%fused_computation.64 | loop fusion | flops 16777216 | bytes 4194308
  115.2 2.7 %copy.36 = bf16[128,64,128]{2,0,1:T(8,128)(2,1)} copy(bf16[128,64,128]{2,1,0:T(8,128)(2,1)S(1)} %bitcast.148) | data formatting | bytes 4194304 | tf_op jit(solution)/shard_map/reshape | solution.py:55
  117.9 4.2 %fusion.16 = bf16[16,8,64,128]{3,1,2,0:T(8,128)(2,1)S(1)} fusion(s32[]{:T(128)S(6)} %select_n.57, bf16[16,8,2048]{2,1,0:T(8,128)(2,1)S(1)} %collective-permute-done.10, bf16[16,8,2048]{2,1,0:T(8,128)(2,1)} %collective-permute-done.9, bf16[16,8,2048]{2,1,0:T(8,128)(2,1)S(1)} %copy-done.12, bf16[16,8,2048]{2,1,0:T(8,128)(2,1)S(1)} %get-tuple-element.232), kind=kLoop, calls=%fused_computation.56 | loop fusion | flops 16777216 | bytes 4194308
  122.7 2.7 %copy.39 = bf16[128,64,128]{2,0,1:T(8,128)(2,1)} copy(bf16[128,64,128]{2,1,0:T(8,128)(2,1)S(1)} %bitcast.149) | data formatting | bytes 4194304 | tf_op jit(solution)/shard_map/reshape | solution.py:55
  125.4 4.3 %fusion.8 = bf16[16,8,64,128]{3,1,2,0:T(8,128)(2,1)S(1)} fusion(s32[]{:T(128)S(6)} %select_n.57, bf16[16,8,2048]{2,1,0:T(8,128)(2,1)S(1)} %collective-permute-done.13, bf16[16,8,2048]{2,1,0:T(8,128)(2,1)} %collective-permute-done.12, bf16[16,8,2048]{2,1,0:T(8,128)(2,1)S(1)} %copy-done.10, bf16[16,8,2048]{2,1,0:T(8,128)(2,1)S(1)} %get-tuple-element.230), kind=kLoop, calls=%fused_computation.48 | loop fusion | flops 16777216 | bytes 4194308
  130.4 2.7 %copy.42 = bf16[128,64,128]{2,0,1:T(8,128)(2,1)} copy(bf16[128,64,128]{2,1,0:T(8,128)(2,1)S(1)} %bitcast.150) | data formatting | bytes 4194304 | tf_op jit(solution)/shard_map/reshape | solution.py:55
  135.3 3.9 %gather_fusion.1 = bf16[64,128,128]{2,1,0:T(8,128)(2,1)} fusion(bf16[128,64,128]{2,0,1:T(8,128)(2,1)} %copy.36, s32[1024]{0:T(1024)S(1)} %pad_clamp_fusion.2), kind=kCustom, calls=%fused_computation.1.clone | custom fusion | bytes 4194560 | tf_op jit(solution)/shard_map/jit(_take)/gather | solution.py:56
  141.4 2.5 %gather_fusion.3 = bf16[64,128,128]{2,1,0:T(8,128)(2,1)S(1)} fusion(bf16[128,64,128]{2,0,1:T(8,128)(2,1)} %copy.42, s32[1024]{0:T(1024)S(1)} %pad_clamp_fusion), kind=kCustom, calls=%fused_computation.3.clone | custom fusion | bytes 4194560 | tf_op jit(solution)/shard_map/jit(_take)/gather | solution.py:56
  144.0 3.1 %fusion.60 = f32[16,128,128]{2,1,0:T(8,128)S(1)} fusion(bf16[4,1,16,4,128,128]{5,4,3,2,1,0:T(8,128)(2,1)} %param.25, bf16[16,4,128,128]{3,2,1,0:T(8,128)(2,1)} %bitcast.153, pred[16,4]{1,0:T(8,128)(4,1)S(1)} %copy.31), kind=kOutput, calls=%fused_computation.100 | convolution fusion | flops 269484032 | bytes 5242944 | tf_op jit(solution)/shard_map/rjkc,jkcd->rjd/dot_general | solution.py:57
  147.1 2.5 %fusion.95 = f32[16,128,128]{2,1,0:T(8,128)S(1)} fusion(f32[16,128,128]{2,1,0:T(8,128)S(1)} %fusion.60, bf16[4,1,16,4,128,128]{5,4,3,2,1,0:T(8,128)(2,1)} %param.25, bf16[16,4,128,128]{3,2,1,0:T(8,128)(2,1)S(1)} %bitcast.154, pred[16,4]{1,0:T(8,128)(4,1)S(1)} %copy.34), kind=kOutput, calls=%fused_computation.107 | convolution fusion | flops 269746176 | bytes 6291520 | tf_op jit(solution)/shard_map/rjkc,jkcd->rjd/dot_general | solution.py:57
  155.4 15.5 %while.18 = (s32[]{:T(128)}, f32[8,2048]{1,0:T(8,128)S(1)}, f32[8,2048]{1,0:T(8,128)S(1)}, bf16[16,8,2048]{2,1,0:T(8,128)(2,1)S(1)}, f32[2048]{0:T(1024)S(1)}, /...) while((s32[]{:T(128)}, f32[8,2048]{1,0:T(8,128)S(1)}, ...), condition=%wide.region_1.4_spmd, body=%wide.region_0.3_spmd.sunk | while | flops 180227 | bytes 581777 | solution.py:23
  (117 shorter events, 36.1 us)
Async XLA Ops:
  0.6 58.9 %copy-start.17 = (s32[4,1,16,4]{2,3,1,0:T(4,128)S(1)}, s32[4,1,16,4]{2,3,1,0:T(4,128)}, u32[]{:S(2)}) copy-start(s32[4,1,16,4]{2,3,1,0:T(4,128)} %param.26) | copy-start | bytes 3076
  0.6 48.9 %collective-permute-start = (bf16[32,8,2048]{2,1,0:T(8,128)(2,1)}, bf16[32,8,2048]{2,1,0:T(8,128)(2,1)}, u32[]{:S(2)}, u32[]{:S(2)}) collective-permute-start(bf16[32,8,2048]{2,1,0:T(8,128)(2,1)} %param.17), channel_id=1, source_target_pairs={{0,4},{4,0},{8,12},{12,8},{1,5},{5,1},{9,13},{13,9},{2,6},{6,2},{1... | collective-permute-start | bytes 3145736 | tf_op jit(solution)/shard_map/ppermute | solution.py:10
  3.7 49.7 %collective-permute-start.4 = (bf16[32,8,2048]{2,1,0:T(8,128)(2,1)}, bf16[32,8,2048]{2,1,0:T(8,128)(2,1)S(1)}, u32[]{:S(2)}, u32[]{:S(2)}) collective-permute-start(bf16[32,8,2048]{2,1,0:T(8,128)(2,1)} %param.17), channel_id=1, source_target_pairs={{0,8},{4,12},{8,0},{12,4},{1,9},{5,13},{9,1},{13,5},{2,10},{6,14},... | collective-permute-start | bytes 3145736 | tf_op jit(solution)/shard_map/ppermute | solution.py:10
  50.8 8.8 %collective-permute-start.1 = (bf16[16,8,2048]{2,1,0:T(8,128)(2,1)S(1)}, bf16[16,8,2048]{2,1,0:T(8,128)(2,1)}, u32[]{:S(2)}, u32[]{:S(2)}) collective-permute-start(bf16[16,8,2048]{2,1,0:T(8,128)(2,1)S(1)} %get-tuple-element.233), channel_id=1, source_target_pairs={{0,1},{1,2},{2,3},{3,0},{4,5},{5,6},{6,7},{7,4},{8,9},{9,10},{10,1... | collective-permute-start | bytes 1572872 | tf_op jit(solution)/shard_map/ppermute | solution.py:48
  53.6 55.6 %copy-start.7 = (bf16[16,8,2048]{2,1,0:T(8,128)(2,1)}, bf16[16,8,2048]{2,1,0:T(8,128)(2,1)S(1)}, u32[]{:S(2)}) copy-start(bf16[16,8,2048]{2,1,0:T(8,128)(2,1)S(1)} %get-tuple-element.231) | copy-start | bytes 1572868
  53.6 11.6 %collective-permute-start.5 = (bf16[16,8,2048]{2,1,0:T(8,128)(2,1)S(1)}, bf16[16,8,2048]{2,1,0:T(8,128)(2,1)}, u32[]{:S(2)}, u32[]{:S(2)}) collective-permute-start(bf16[16,8,2048]{2,1,0:T(8,128)(2,1)S(1)} %get-tuple-element.231), channel_id=1, source_target_pairs={{0,1},{1,2},{2,3},{3,0},{4,5},{5,6},{6,7},{7,4},{8,9},{9,10},{10,1... | collective-permute-start | bytes 1572872 | tf_op jit(solution)/shard_map/ppermute | solution.py:48
  55.4 15.3 %collective-permute-start.8 = (bf16[16,8,2048]{2,1,0:T(8,128)(2,1)S(1)}, bf16[16,8,2048]{2,1,0:T(8,128)(2,1)S(1)}, u32[]{:S(2)}, u32[]{:S(2)}) collective-permute-start(bf16[16,8,2048]{2,1,0:T(8,128)(2,1)S(1)} %get-tuple-element.232), channel_id=1, source_target_pairs={{0,1},{1,2},{2,3},{3,0},{4,5},{5,6},{6,7},{7,4},{8,9},{9,10},{10,1... | collective-permute-start | bytes 1572872 | tf_op jit(solution)/shard_map/ppermute | solution.py:48
  55.5 20.8 %collective-permute-start.11 = (bf16[16,8,2048]{2,1,0:T(8,128)(2,1)S(1)}, bf16[16,8,2048]{2,1,0:T(8,128)(2,1)S(1)}, u32[]{:S(2)}, u32[]{:S(2)}) collective-permute-start(bf16[16,8,2048]{2,1,0:T(8,128)(2,1)S(1)} %get-tuple-element.230), channel_id=1, source_target_pairs={{0,1},{1,2},{2,3},{3,0},{4,5},{5,6},{6,7},{7,4},{8,9},{9,10},{10,1... | collective-permute-start | bytes 1572872 | tf_op jit(solution)/shard_map/ppermute | solution.py:48
  59.6 22.5 %collective-permute-start.2 = (bf16[16,8,2048]{2,1,0:T(8,128)(2,1)}, bf16[16,8,2048]{2,1,0:T(8,128)(2,1)}, u32[]{:S(2)}, u32[]{:S(2)}) collective-permute-start(bf16[16,8,2048]{2,1,0:T(8,128)(2,1)} %collective-permute-done.1), channel_id=1, source_target_pairs={{0,1},{1,2},{2,3},{3,0},{4,5},{5,6},{6,7},{7,4},{8,9},{9,10},{10,1... | collective-permute-start | bytes 1572872 | tf_op jit(solution)/shard_map/ppermute | solution.py:48
  65.2 22.5 %collective-permute-start.6 = (bf16[16,8,2048]{2,1,0:T(8,128)(2,1)}, bf16[16,8,2048]{2,1,0:T(8,128)(2,1)}, u32[]{:S(2)}, u32[]{:S(2)}) collective-permute-start(bf16[16,8,2048]{2,1,0:T(8,128)(2,1)} %collective-permute-done.5), channel_id=1, source_target_pairs={{0,1},{1,2},{2,3},{3,0},{4,5},{5,6},{6,7},{7,4},{8,9},{9,10},{10,1... | collective-permute-start | bytes 1572872 | tf_op jit(solution)/shard_map/ppermute | solution.py:48
  70.7 38.5 %copy-start.11 = (bf16[16,8,2048]{2,1,0:T(8,128)(2,1)}, bf16[16,8,2048]{2,1,0:T(8,128)(2,1)S(1)}, u32[]{:S(2)}) copy-start(bf16[16,8,2048]{2,1,0:T(8,128)(2,1)S(1)} %collective-permute-done.8) | copy-start | bytes 1572868
  70.7 22.6 %collective-permute-start.9 = (bf16[16,8,2048]{2,1,0:T(8,128)(2,1)S(1)}, bf16[16,8,2048]{2,1,0:T(8,128)(2,1)}, u32[]{:S(2)}, u32[]{:S(2)}) collective-permute-start(bf16[16,8,2048]{2,1,0:T(8,128)(2,1)S(1)} %collective-permute-done.8), channel_id=1, source_target_pairs={{0,1},{1,2},{2,3},{3,0},{4,5},{5,6},{6,7},{7,4},{8,9},{9,10},{10,1... | collective-permute-start | bytes 1572872 | tf_op jit(solution)/shard_map/ppermute | solution.py:48
  76.3 32.9 %copy-start.9 = (bf16[16,8,2048]{2,1,0:T(8,128)(2,1)}, bf16[16,8,2048]{2,1,0:T(8,128)(2,1)S(1)}, u32[]{:S(2)}) copy-start(bf16[16,8,2048]{2,1,0:T(8,128)(2,1)S(1)} %collective-permute-done.11) | copy-start | bytes 1572868
  76.3 22.6 %collective-permute-start.12 = (bf16[16,8,2048]{2,1,0:T(8,128)(2,1)S(1)}, bf16[16,8,2048]{2,1,0:T(8,128)(2,1)}, u32[]{:S(2)}, u32[]{:S(2)}) collective-permute-start(bf16[16,8,2048]{2,1,0:T(8,128)(2,1)S(1)} %collective-permute-done.11), channel_id=1, source_target_pairs={{0,1},{1,2},{2,3},{3,0},{4,5},{5,6},{6,7},{7,4},{8,9},{9,10},{10,1... | collective-permute-start | bytes 1572872 | tf_op jit(solution)/shard_map/ppermute | solution.py:48
  82.0 22.5 %collective-permute-start.3 = (bf16[16,8,2048]{2,1,0:T(8,128)(2,1)}, bf16[16,8,2048]{2,1,0:T(8,128)(2,1)}, u32[]{:S(2)}, u32[]{:S(2)}) collective-permute-start(bf16[16,8,2048]{2,1,0:T(8,128)(2,1)} %collective-permute-done.2), channel_id=1, source_target_pairs={{0,1},{1,2},{2,3},{3,0},{4,5},{5,6},{6,7},{7,4},{8,9},{9,10},{10,1... | collective-permute-start | bytes 1572872 | tf_op jit(solution)/shard_map/ppermute | solution.py:48
  87.7 22.9 %collective-permute-start.7 = (bf16[16,8,2048]{2,1,0:T(8,128)(2,1)}, bf16[16,8,2048]{2,1,0:T(8,128)(2,1)S(1)}, u32[]{:S(2)}, u32[]{:S(2)}) collective-permute-start(bf16[16,8,2048]{2,1,0:T(8,128)(2,1)} %collective-permute-done.6), channel_id=1, source_target_pairs={{0,1},{1,2},{2,3},{3,0},{4,5},{5,6},{6,7},{7,4},{8,9},{9,10},{10,1... | collective-permute-start | bytes 1572872 | tf_op jit(solution)/shard_map/ppermute | solution.py:48
  93.3 24.6 %collective-permute-start.10 = (bf16[16,8,2048]{2,1,0:T(8,128)(2,1)}, bf16[16,8,2048]{2,1,0:T(8,128)(2,1)S(1)}, u32[]{:S(2)}, u32[]{:S(2)}) collective-permute-start(bf16[16,8,2048]{2,1,0:T(8,128)(2,1)} %collective-permute-done.9), channel_id=1, source_target_pairs={{0,1},{1,2},{2,3},{3,0},{4,5},{5,6},{6,7},{7,4},{8,9},{9,10},{10,1... | collective-permute-start | bytes 1572872 | tf_op jit(solution)/shard_map/ppermute | solution.py:48
  98.9 26.5 %collective-permute-start.13 = (bf16[16,8,2048]{2,1,0:T(8,128)(2,1)}, bf16[16,8,2048]{2,1,0:T(8,128)(2,1)S(1)}, u32[]{:S(2)}, u32[]{:S(2)}) collective-permute-start(bf16[16,8,2048]{2,1,0:T(8,128)(2,1)} %collective-permute-done.12), channel_id=1, source_target_pairs={{0,1},{1,2},{2,3},{3,0},{4,5},{5,6},{6,7},{7,4},{8,9},{9,10},{10,1... | collective-permute-start | bytes 1572872 | tf_op jit(solution)/shard_map/ppermute | solution.py:48
  109.2 1.4 copy-start.8
  114.6 3.4 %copy-start.12 = (bf16[16,8,2048]{2,1,0:T(8,128)(2,1)S(1)}, bf16[16,8,2048]{2,1,0:T(8,128)(2,1)}, u32[]{:S(2)}) copy-start(bf16[16,8,2048]{2,1,0:T(8,128)(2,1)} %copy-done.11) | copy-start | bytes 1572868
  122.1 3.3 %copy-start.10 = (bf16[16,8,2048]{2,1,0:T(8,128)(2,1)S(1)}, bf16[16,8,2048]{2,1,0:T(8,128)(2,1)}, u32[]{:S(2)}) copy-start(bf16[16,8,2048]{2,1,0:T(8,128)(2,1)} %copy-done.9) | copy-start | bytes 1572868
  135.3 4.0 %copy-start = (bf16[128,64,128]{2,0,1:T(8,128)(2,1)S(1)}, bf16[128,64,128]{2,0,1:T(8,128)(2,1)}, u32[]{:S(2)}) copy-start(bf16[128,64,128]{2,0,1:T(8,128)(2,1)} %copy.39) | copy-start | bytes 6291460
  144.0 3.1 %copy-start.6 = (bf16[64,128,128]{2,1,0:T(8,128)(2,1)S(1)}, bf16[64,128,128]{2,1,0:T(8,128)(2,1)}, u32[]{:S(2)}) copy-start(bf16[64,128,128]{2,1,0:T(8,128)(2,1)} %gather_fusion.1) | copy-start | bytes 6291460
  147.1 2.6 %copy-start.5 = (bf16[64,128,128]{2,1,0:T(8,128)(2,1)S(1)}, bf16[64,128,128]{2,1,0:T(8,128)(2,1)}, u32[]{:S(2)}) copy-start(bf16[64,128,128]{2,1,0:T(8,128)(2,1)} %gather_fusion.2) | copy-start | bytes 6291460
  (8 other events, 6.6 us)
